TPU v7x, 32 devices: a whole 2x2x4 slice. The times are simulated.
32 devices in a mesh: narrow: 4 (over y, core), wide: 8 (over z, x).
Axes of the slice: x: 2, y: 2, z: 4, core: 2. Of those that a mesh axis runs over, the one named last changes fastest.
Arguments:
- hidden_in: bfloat16 [256, 16384], P('narrow', 'wide'), may hold values from -6 to 6
- w_query: bfloat16 [16384, 8, 2048], P('wide', 'narrow'), may hold values from -0.046875 to 0.046875
- w_keyval: bfloat16 [16384, 8, 256], P('wide', 'narrow'), may hold values from -0.046875 to 0.046875
- w_out: bfloat16 [16384, 16384], P('narrow', 'wide'), may hold values from -0.125 to 0.125
- key_cache: bfloat16 [256, 8, 1024, 128], P('wide', 'narrow'), may hold values from -1300 to 1300
- value_cache: bfloat16 [256, 8, 1024, 128], P('wide', 'narrow'), may hold values from -6 to 6
- lengths: int32 [256], P('wide'), may hold values from 2 to 1024, as said below
Outputs:
- hidden_out: bfloat16 [256, 16384], P('narrow', 'wide')
Inputs may be any that keep to these rules, and one draw needn't show every extreme that they name: `lengths`: each row holds at least 2 cached tokens; some row holds exactly 1024.
All inputs are finite; a program needn't handle non-finite values.
Results may differ from a plain program's by a relative error of at most 0.019.
The roundings to bfloat16 on the way count: a program that leaves them out, or rounds other values in their place, can miss the bound.
Values may be sent and summed in bfloat16 or wider, within the bound.
No kernel may reach another device: no remote copies, remote signals or barrier semaphores. Data moves between devices by JAX's collectives and lax.ppermute only.
A program may use at most 192 MiB of HBM per device.

v0:
```python
import jax
import jax.numpy as jnp
from jax import lax
from jax.sharding import PartitionSpec as P

STEPS = 2
rope_base = 500000.0


def rope(values, position):
    half = values.shape[-1] // 2
    freq = rope_base ** (-2.0 * jnp.arange(half, dtype=jnp.float32) / values.shape[-1])
    angle = position.astype(jnp.float32)[:, None] * freq[None, :]
    shape = (angle.shape[0],) + (1,) * (values.ndim - 2) + (half,)
    cosine = jnp.cos(angle).reshape(shape)
    sine = jnp.sin(angle).reshape(shape)
    first = values[..., :half]
    second = values[..., half:]
    return jnp.concatenate(
        (first * cosine - second * sine, second * cosine + first * sine), axis=-1
    )


def attend_step(
    every, step, w_q2, w_kv2, w_out, key_cache, value_cache, lengths, new_keys, new_vals
):
    local_rows = key_cache.shape[0]
    groups = key_cache.shape[1]
    slots = key_cache.shape[2]
    head_dim = key_cache.shape[3]
    qcols = w_q2.shape[1]
    per_group = qcols // (groups * head_dim)
    part_q = jnp.dot(every, w_q2, preferred_element_type=jnp.float32)
    part_kv = jnp.dot(every, w_kv2, preferred_element_type=jnp.float32)
    proj = lax.psum_scatter(
        jnp.concatenate((part_q, part_kv), axis=1), "wide", scatter_dimension=0, tiled=True
    )
    position = lengths + step
    query = rope(proj[:, :qcols].reshape(local_rows, groups, per_group, head_dim), position).astype(
        jnp.bfloat16
    )
    kv = proj[:, qcols:].reshape(local_rows, groups, 2 * head_dim)
    new_keys.append(rope(kv[:, :, :head_dim], position).astype(jnp.bfloat16))
    new_vals.append(kv[:, :, head_dim:].astype(jnp.bfloat16))
    keys_now = jnp.stack(new_keys, axis=2)
    vals_now = jnp.stack(new_vals, axis=2)
    scale = 1.0 / head_dim**0.5
    live = (jnp.arange(slots, dtype=jnp.int32)[None, :] < lengths[:, None])[:, None, None, :]
    cached = (
        jnp.einsum("rgjd,rgcd->rgjc", query, key_cache, preferred_element_type=jnp.float32) * scale
    )
    cached = jnp.where(live, cached, -1e30)
    fresh = (
        jnp.einsum("rgjd,rgsd->rgjs", query, keys_now, preferred_element_type=jnp.float32) * scale
    )
    top = jnp.maximum(jnp.max(cached, axis=-1), jnp.max(fresh, axis=-1))
    e_cached = jnp.where(live, jnp.exp(cached - top[..., None]), 0.0)
    e_fresh = jnp.exp(fresh - top[..., None])
    total = jnp.sum(e_cached, axis=-1) + jnp.sum(e_fresh, axis=-1)
    p_cached = (e_cached / total[..., None]).astype(jnp.bfloat16)
    p_fresh = (e_fresh / total[..., None]).astype(jnp.bfloat16)
    out = jnp.einsum("rgjc,rgcd->rgjd", p_cached, value_cache, preferred_element_type=jnp.float32)
    out = out + jnp.einsum("rgjs,rgsd->rgjd", p_fresh, vals_now, preferred_element_type=jnp.float32)
    attended = out.astype(jnp.bfloat16).reshape(local_rows, groups * per_group * head_dim)
    return jnp.dot(
        jnp.concatenate(
            [
                lax.all_gather(attended[:, i * 1024 : (i + 1) * 1024], "wide", axis=0, tiled=True)
                for i in range(attended.shape[1] // 1024)
            ],
            axis=1,
        ),
        w_out,
        preferred_element_type=jnp.float32,
    )


def narrow_gather(state, n_narrow):
    rows, cols = state.shape
    half = rows // 2
    parts = [
        lax.all_gather(state[h * half : (h + 1) * half], "narrow", axis=0, tiled=True).reshape(
            n_narrow, 1, half, cols
        )
        for h in range(2)
    ]
    return jnp.concatenate(parts, axis=1).reshape(n_narrow * rows, cols)


def on_device(hidden_in, w_query, w_keyval, w_out, key_cache, value_cache, lengths):
    w_q2 = w_query.reshape(w_query.shape[0], -1)
    w_kv2 = w_keyval.reshape(w_keyval.shape[0], -1)
    new_keys = []
    new_vals = []
    result = hidden_in
    for step in range(STEPS):
        partial_value = attend_step(
            (
                lax.all_gather(result, "narrow", axis=0, tiled=True)
                if step == 0
                else narrow_gather(result, lax.axis_size("narrow"))
            ),
            step,
            w_q2,
            w_kv2,
            w_out,
            key_cache,
            value_cache,
            lengths,
            new_keys,
            new_vals,
        )
        update = lax.psum_scatter(partial_value, "narrow", scatter_dimension=0, tiled=True)
        result = (result.astype(jnp.float32) + update).astype(jnp.bfloat16)
    return result


def solution(mesh):
    placed = (
        P("narrow", "wide"),
        P("wide", "narrow", None),
        P("wide", "narrow", None),
        P("narrow", "wide"),
        P("wide", "narrow", None, None),
        P("wide", "narrow", None, None),
        P("wide"),
    )
    return jax.shard_map(
        on_device, mesh=mesh, in_specs=placed, out_specs=P("narrow", "wide"), check_vma=False
    )
```

profile of v0, /device:TPU:0, one launch (start us, length us, event | category | flops | bytes accessed | tf_op | source)
XLA Modules:
  0.0 656.7 jit_solution(6499864838221455631)
XLA Ops:
  6.5 0.7 all-gather.2.cloned.1.call-update
  7.3 0.0 reduce-scatter.5.cloned.1.call-start
  7.3 17.5 %copy.69 = bf16[256,8,2,2048]{3,1,2,0:T(8,128)(2,1)} copy(bf16[256,8,2,2048]{3,2,1,0:T(2,128)(2,1)} %bitcast.62) | data formatting | bytes 33554432
  24.8 0.5 copy.70
  25.3 3.1 all-gather.2.cloned.1.call-done
  28.4 10.5 %fusion.80 = f32[256,4096]{1,0:T(8,128)S(1)} fusion(bf16[256,2048]{1,0:T(8,128)(2,1)} %all-gather.2.cloned.1.call-done, bf16[2048,4096]{1,0:T(8,128)(2,1)} %bitcast.63), kind=kOutput, calls=%fused_computation.122 | convolution fusion | flops 4294967296 | bytes 22020096 | tf_op jit(solution)/shard_map/dot_general | solution.py:33
  38.9 0.7 fusion.81
  39.6 2.5 pad_maximum_fusion
  42.1 0.0 reduce-scatter.5.cloned.1.call-update
  42.2 0.0 reduce-scatter.7.cloned.1.call-start
  42.2 0.6 copy-done.4
  42.8 0.1 iota_compare_fusion
  42.9 0.2 multiply_cosine_fusion
  43.1 94.6 %reduce-scatter.5.cloned.1.call-done = f32[32,4608]{1,0:T(8,128)} async-done(((f32[256,4608]{1,0:T(8,128)}), f32[32,4608]{1,0:T(8,128)}) %reduce-scatter.5.cloned.1.call-update) | async-done | bytes 589840 | tf_op jit(solution)/shard_map/reduce_scatter | solution.py:35
  137.7 0.8 slice.107
  138.6 0.1 fusion.78
  138.7 1.1 slice_bitcast_fusion.1
  139.8 0.1 copy.71
  139.9 0.2 subtract_convert_fusion.1
  140.1 0.1 maximum_bitcast_fusion
  140.2 0.3 fusion.38
  140.5 12.2 %fusion = (f32[32,2,16]{2,1,0:T(2,128)S(1)}, f32[32,2,16,1024]{3,2,1,0:T(8,128)}) fusion(pred[32,1024]{1,0:T(8,128)(4,1)S(1)} %iota_compare_fusion, bf16[32,2,1024,128]{3,2,1,0:T(8,128)(2,1)} %param.11, bf16[32,2,16,64]{3,2,1,0:T(8,128)(2,1)S(1)} %get-tuple-element.8, bf16[32,2,16,64]{3,2,1,0:T(8,128)(2,1)S(1)} %get-tuple-element.7), kind=kOutput, calls=%fused_computation.8 | convolution fusion | flops 272104448 | bytes 21270528 | tf_op jit(solution)/shard_map/rgjd,rgcd->rgjc/dot_general | solution.py:50
  152.8 3.8 fusion.2
  156.6 0.1 fusion.57
  156.7 7.5 %fusion.35 = bf16[32,2,16,128]{3,2,1,0:T(8,128)(2,1)S(1)} fusion(bf16[32,2,1024,128]{3,2,1,0:T(8,128)(2,1)} %param.12, f32[32,2,16,1024]{3,2,1,0:T(8,128)S(1)} %copy-done.1, f32[32,2,16]{2,1,0:T(2,128)S(1)} %get-tuple-element.22, f32[32,2,16]{2,1,0:T(2,128)S(1)} %multiply_maximum_fusion, pred[32,1024]{1,0:T(8,128)(4,1)S(1)} %iota_compare_fusion, ...), kind=kOutput, calls=%fused_computation.44 | convolution fusion | flops 275120128 | bytes 21311488 | tf_op jit(solution)/shard_map/rgjc,rgcd->rgjd/dot_general | solution.py:62
  164.2 0.1 copy.104
  164.4 31.5 %all_gather.34 = bf16[256,1024]{1,0:T(8,128)(2,1)S(1)} all-gather(bf16[32,1024]{1,0:T(8,128)(2,1)S(1)} %get-tuple-element.15), channel_id=1, replica_groups=mesh['narrow'=4,'wide'=8] {'wide'}, dimensions={0}, use_global_device_ids=true | all-gather | bytes 589824 | tf_op jit(solution)/shard_map/all_gather | solution.py:68
  195.9 31.4 %all_gather.35 = bf16[256,1024]{1,0:T(8,128)(2,1)S(1)} all-gather(bf16[32,1024]{1,0:T(8,128)(2,1)S(1)} %get-tuple-element.18), channel_id=1, replica_groups=mesh['narrow'=4,'wide'=8] {'wide'}, dimensions={0}, use_global_device_ids=true | all-gather | bytes 589824 | tf_op jit(solution)/shard_map/all_gather | solution.py:68
  227.2 31.5 %all_gather.36 = bf16[256,1024]{1,0:T(8,128)(2,1)S(1)} all-gather(bf16[32,1024]{1,0:T(8,128)(2,1)S(1)} %get-tuple-element.17), channel_id=1, replica_groups=mesh['narrow'=4,'wide'=8] {'wide'}, dimensions={0}, use_global_device_ids=true | all-gather | bytes 589824 | tf_op jit(solution)/shard_map/all_gather | solution.py:68
  258.7 31.2 %all_gather.37 = bf16[256,1024]{1,0:T(8,128)(2,1)S(1)} all-gather(bf16[32,1024]{1,0:T(8,128)(2,1)S(1)} %get-tuple-element.16), channel_id=1, replica_groups=mesh['narrow'=4,'wide'=8] {'wide'}, dimensions={0}, use_global_device_ids=true | all-gather | bytes 589824 | tf_op jit(solution)/shard_map/all_gather | solution.py:68
  289.9 10.2 %fusion.6 = f32[256,2048]{1,0:T(8,128)} fusion(bf16[4096,2048]{1,0:T(8,128)(2,1)} %param.10, bf16[256,1024]{1,0:T(8,128)(2,1)S(1)} %all_gather.37, bf16[256,1024]{1,0:T(8,128)(2,1)S(1)} %all_gather.36, bf16[256,1024]{1,0:T(8,128)(2,1)S(1)} %all_gather.35, bf16[256,1024]{1,0:T(8,128)(2,1)S(1)} %all_gather.34), kind=kOutput, calls=%fused_computation.14 | convolution fusion | flops 4303355904 | bytes 20971520 | tf_op jit(solution)/shard_map/dot_general | solution.py:65
  300.1 0.0 reduce-scatter.7.cloned.1.call-update
  300.1 0.0 reduce-scatter.9.cloned.1.call-start
  300.2 31.1 %reduce-scatter.7.cloned.1.call-done = f32[64,2048]{1,0:T(8,128)} async-done(((f32[256,2048]{1,0:T(8,128)}), f32[64,2048]{1,0:T(8,128)}) %reduce-scatter.7.cloned.1.call-update) | async-done | bytes 524304 | tf_op jit(solution)/shard_map/reduce_scatter | solution.py:113
  331.3 1.1 add_convert_fusion.2
  332.4 6.8 %all_gather.38 = bf16[128,2048]{1,0:T(8,128)(2,1)S(1)} all-gather(bf16[32,2048]{1,0:T(8,128)(2,1)S(1)} %get-tuple-element.13), channel_id=1, replica_groups=mesh['narrow'=4,'wide'=8] {'narrow'}, dimensions={0}, use_global_device_ids=true | all-gather | bytes 655360 | tf_op jit(solution)/shard_map/all_gather | solution.py:82
  339.2 7.3 %all_gather.39 = bf16[128,2048]{1,0:T(8,128)(2,1)S(1)} all-gather(bf16[32,2048]{1,0:T(8,128)(2,1)S(1)} %get-tuple-element.14), channel_id=1, replica_groups=mesh['narrow'=4,'wide'=8] {'narrow'}, dimensions={0}, use_global_device_ids=true | all-gather | bytes 655360 | tf_op jit(solution)/shard_map/all_gather | solution.py:82
  346.5 0.1 pad_maximum_fusion.2
  346.6 8.2 %fusion.82 = f32[256,4096]{1,0:T(8,128)S(1)} fusion(bf16[256,2048]{1,0:T(8,128)(2,1)S(1)} %bitcast.72, bf16[2048,4096]{1,0:T(8,128)(2,1)} %bitcast.64), kind=kOutput, calls=%fused_computation.124 | convolution fusion | flops 4294967296 | bytes 22020096 | tf_op jit(solution)/shard_map/dot_general | solution.py:33
  354.7 0.7 fusion.83
  355.5 2.5 pad_maximum_fusion.1
  358.0 0.0 reduce-scatter.9.cloned.1.call-update
  358.0 0.0 reduce-scatter.11.cloned.1.call-start
  358.2 95.8 %reduce-scatter.9.cloned.1.call-done = f32[32,4608]{1,0:T(8,128)} async-done(((f32[256,4608]{1,0:T(8,128)}), f32[32,4608]{1,0:T(8,128)}) %reduce-scatter.9.cloned.1.call-update) | async-done | bytes 589840 | tf_op jit(solution)/shard_map/reduce_scatter | solution.py:35
  454.0 0.8 slice.120
  454.9 0.1 fusion.77
  455.1 1.1 slice_bitcast_fusion
  456.2 0.1 copy.73
  456.3 0.2 subtract_convert_fusion
  456.5 12.2 %fusion.1 = (f32[32,2,16]{2,1,0:T(2,128)S(1)}, f32[32,2,16,1024]{3,2,1,0:T(8,128)}) fusion(pred[32,1024]{1,0:T(8,128)(4,1)S(1)} %iota_compare_fusion, bf16[32,2,1024,128]{3,2,1,0:T(8,128)(2,1)} %param.11, bf16[32,2,16,64]{3,2,1,0:T(8,128)(2,1)S(1)} %get-tuple-element.6, bf16[32,2,16,64]{3,2,1,0:T(8,128)(2,1)S(1)} %get-tuple-element.5), kind=kOutput, calls=%fused_computation.9 | convolution fusion | flops 272104448 | bytes 21270528 | tf_op jit(solution)/shard_map/rgjd,rgcd->rgjc/dot_general | solution.py:50
  468.7 0.5 fusion.79
  469.3 0.1 fusion.40
  469.4 3.9 fusion.3
  473.4 7.3 %fusion.5 = f32[32,2,16,128]{3,2,1,0:T(8,128)S(1)} fusion(bf16[32,2,1024,128]{3,2,1,0:T(8,128)(2,1)} %param.12, f32[32,2,16,1024]{3,2,1,0:T(8,128)S(1)} %copy-done, f32[32,2,16]{2,1,0:T(2,128)S(1)} %add.59, f32[32,2,16]{2,1,0:T(2,128)S(1)} %max.13, pred[32,1024]{1,0:T(8,128)(4,1)S(1)} %iota_compare_fusion), kind=kOutput, calls=%fused_computation.13 | convolution fusion | flops 274726912 | bytes 21536768 | tf_op jit(solution)/shard_map/rgjc,rgcd->rgjd/dot_general | solution.py:62
  480.8 0.3 fusion.36
  481.1 0.1 copy.103
  481.2 31.5 %all_gather.40 = bf16[256,1024]{1,0:T(8,128)(2,1)S(1)} all-gather(bf16[32,1024]{1,0:T(8,128)(2,1)S(1)} %get-tuple-element.9), channel_id=1, replica_groups=mesh['narrow'=4,'wide'=8] {'wide'}, dimensions={0}, use_global_device_ids=true | all-gather | bytes 589824 | tf_op jit(solution)/shard_map/all_gather | solution.py:68
  512.7 31.3 %all_gather.41 = bf16[256,1024]{1,0:T(8,128)(2,1)S(1)} all-gather(bf16[32,1024]{1,0:T(8,128)(2,1)S(1)} %get-tuple-element.12), channel_id=1, replica_groups=mesh['narrow'=4,'wide'=8] {'wide'}, dimensions={0}, use_global_device_ids=true | all-gather | bytes 589824 | tf_op jit(solution)/shard_map/all_gather | solution.py:68
  544.1 31.6 %all_gather.42 = bf16[256,1024]{1,0:T(8,128)(2,1)S(1)} all-gather(bf16[32,1024]{1,0:T(8,128)(2,1)S(1)} %get-tuple-element.11), channel_id=1, replica_groups=mesh['narrow'=4,'wide'=8] {'wide'}, dimensions={0}, use_global_device_ids=true | all-gather | bytes 589824 | tf_op jit(solution)/shard_map/all_gather | solution.py:68
  575.7 31.2 %all_gather.43 = bf16[256,1024]{1,0:T(8,128)(2,1)S(1)} all-gather(bf16[32,1024]{1,0:T(8,128)(2,1)S(1)} %get-tuple-element.10), channel_id=1, replica_groups=mesh['narrow'=4,'wide'=8] {'wide'}, dimensions={0}, use_global_device_ids=true | all-gather | bytes 589824 | tf_op jit(solution)/shard_map/all_gather | solution.py:68
  606.8 10.2 %fusion.14 = f32[256,2048]{1,0:T(8,128)} fusion(bf16[4096,2048]{1,0:T(8,128)(2,1)} %param.10, bf16[256,1024]{1,0:T(8,128)(2,1)S(1)} %all_gather.43, bf16[256,1024]{1,0:T(8,128)(2,1)S(1)} %all_gather.42, bf16[256,1024]{1,0:T(8,128)(2,1)S(1)} %all_gather.41, bf16[256,1024]{1,0:T(8,128)(2,1)S(1)} %all_gather.40), kind=kOutput, calls=%fused_computation.22 | convolution fusion | flops 4303355904 | bytes 20971520 | tf_op jit(solution)/shard_map/dot_general | solution.py:65
  617.0 0.0 reduce-scatter.11.cloned.1.call-update
  617.0 31.4 %reduce-scatter.11.cloned.1.call-done = f32[64,2048]{1,0:T(8,128)} async-done(((f32[256,2048]{1,0:T(8,128)}), f32[64,2048]{1,0:T(8,128)}) %reduce-scatter.11.cloned.1.call-update) | async-done | bytes 524304 | tf_op jit(solution)/shard_map/reduce_scatter | solution.py:113
  648.4 1.8 add_convert_fusion
  (35 shorter events, 0.5 us)
Async XLA Ops:
  6.5 21.8 %all-gather.2.cloned.1.call-start = ((), (), s32[]{:S(2)}) async-start(), calls=%async_computation.4 | async-start | bytes 1310720 | tf_op jit(solution)/shard_map/all_gather | solution.py:99
  7.3 130.4 %reduce-scatter.5.cloned.1.call-start = ((), (), s32[]{:S(2)}) async-start(), calls=%async_computation.5 | async-start | bytes 5308416 | tf_op jit(solution)/shard_map/reduce_scatter | solution.py:35
  7.3 17.5 %copy-start.2 = (bf16[2048,2,256]{2,1,0:T(2,128)(2,1)S(1)}, bf16[2048,2,256]{2,1,0:T(2,128)(2,1)}, u32[]{:S(2)}) copy-start(bf16[2048,2,256]{2,1,0:T(2,128)(2,1)} %param.9) | copy-start | bytes 6291460
  28.4 10.5 %copy-start.5 = (bf16[256,2048]{1,0:T(8,128)(2,1)S(1)}, bf16[256,2048]{1,0:T(8,128)(2,1)}, u32[]{:S(2)}) copy-start(bf16[256,2048]{1,0:T(8,128)(2,1)} %all-gather.2.cloned.1.call-done) | copy-start | bytes 3145732
  42.1 0.7 copy-start.4
  42.2 289.1 %reduce-scatter.7.cloned.1.call-start = ((), (), s32[]{:S(2)}) async-start(), calls=%async_computation.6 | async-start | bytes 2621440 | tf_op jit(solution)/shard_map/reduce_scatter | solution.py:113
  152.8 3.9 copy-start.1
  289.9 41.4 %copy-start.3 = (bf16[64,2048]{1,0:T(8,128)(2,1)S(1)}, bf16[64,2048]{1,0:T(8,128)(2,1)}, u32[]{:S(2)}) copy-start(bf16[64,2048]{1,0:T(8,128)(2,1)} %param.7) | copy-start | bytes 786436
  300.1 153.8 %reduce-scatter.9.cloned.1.call-start = ((), (), s32[]{:S(2)}) async-start(), calls=%async_computation.7 | async-start | bytes 5308416 | tf_op jit(solution)/shard_map/reduce_scatter | solution.py:35
  358.0 290.4 %reduce-scatter.11.cloned.1.call-start = ((), (), s32[]{:S(2)}) async-start(), calls=%async_computation.8 | async-start | bytes 2621440 | tf_op jit(solution)/shard_map/reduce_scatter | solution.py:113
  468.7 4.7 copy-start
Sparse Core Ops, SparseCore 0:
  8.9 19.4 all-gather.1
  42.3 95.3 reduce-scatter.4
  300.3 30.9 reduce-scatter.6
  358.1 95.7 reduce-scatter.8
  617.2 31.1 reduce-scatter.10
where the time goes:
time: 657 us
  blocking collectives  265 us (40%)
  waiting for transfers between devices  257 us (39%)
  matrix products  80.9 us (12%)
  local copies, waits for them, and re-layouts  23.4 us (4%)
  other arithmetic  16.9 us (3%)
  between operations  13.5 us (2%)
    all_gather x8, blocking collectives, attend_step(): lax.all_gather(attended[:, i * 1024:(i + 1) * 1024], 'wide', axis=0, tile...  251 us
    reduce_scatter x2, waiting for transfers between devices, attend_step(): lax.psum_scatter(jnp.concatenate((part_q, part_kv), axis=1), 'wide', scat...  190 us
    reduce_scatter x2, waiting for transfers between devices, on_device(): lax.psum_scatter(partial_value, 'narrow', scatter_dimension=0, tiled=True)  62.4 us
    dot_general x2, matrix products, attend_step(): jnp.einsum('rgjd,rgcd->rgjc', query, key_cache, preferred_element_type=jn...  24.5 us
    unnamed x21, local copies, waits for them, and re-layouts  21.2 us
    dot_general x2, matrix products, attend_step(): jnp.dot(jnp.concatenate([lax.all_gather(attended[:, i * 1024:(i + 1) * 10...  20.4 us
    dot_general x2, matrix products, attend_step(): part_q = jnp.dot(every, w_q2, preferred_element_type=jnp.float32)  18.6 us
    dot_general x2, matrix products, attend_step(): jnp.einsum('rgjc,rgcd->rgjd', p_cached, value_cache, preferred_element_ty...  14.8 us
  transfers between devices with their start and end apart: 5, of which 5 were waited for; matrix products, arithmetic and copies ran while one was open for 3% of the time, Pallas kernels for 0%

commit v1 on v0

--- a/solution.py
+++ b/solution.py
@@ -5,6 +5,18 @@
 
 STEPS = 2
 rope_base = 500000.0
+
+
+def doubled_up(shard, axis, dim):
+    ways, here, step = (lax.axis_size(axis), lax.axis_index(axis), shard.shape[dim])
+    line, have = (shard, 1)
+    while have < ways:
+        line = jnp.concatenate(
+            [line, lax.ppermute(line, axis, [(d, (d - have) % ways) for d in range(ways)])],
+            axis=dim,
+        )
+        have = 2 * have
+    return jnp.roll(line, here * step, axis=dim)
 
 
 def rope(values, position):
@@ -65,7 +77,7 @@
     return jnp.dot(
         jnp.concatenate(
             [
-                lax.all_gather(attended[:, i * 1024 : (i + 1) * 1024], "wide", axis=0, tiled=True)
+                doubled_up(attended[:, i * 1024 : (i + 1) * 1024], "wide", 0)
                 for i in range(attended.shape[1] // 1024)
             ],
             axis=1,

time: 657 us -> 552 us (0.84); the launches traced: 657 us -> 543 us
  blocking collectives: 265 us -> 14.2 us
  waiting for transfers between devices: 257 us -> 325 us
  starting transfers between devices: 0.17 us -> 54 us
  other arithmetic: 16.9 us -> 31.8 us
    all_gather x8 -> x0, blocking collectives: 251 us -> none  [attend_step(): lax.all_gather(attended[:, i * 1024:(i + 1) * 1024], 'wide', axis=0, tile...]
    ppermute x0 -> x24, waiting for transfers between devices: none -> 67.1 us  [doubled_up(): lax.ppermute(line, axis, [(d, (d - have) % ways) for d in range(ways)])]
    ppermute x0 -> x24, starting transfers between devices: none -> 53.8 us  [doubled_up(): lax.ppermute(line, axis, [(d, (d - have) % ways) for d in range(ways)])]
    concatenate x0 -> x24, other arithmetic: none -> 14.9 us  [the longest x8 14.6 us: doubled_up(): return jnp.roll(line, here * step, axis=dim)]
  transfers between devices with their start and end apart: 5 -> 29, of which waited for: 5 -> 21; matrix products, arithmetic and copies ran while one was open for 3% -> 5% of each run, Pallas kernels for 0% -> 0%
where the time goes in v1:
time: 552 us; the launch traced here: 543 us
  waiting for transfers between devices  325 us (59%)
  matrix products  81 us (15%)
  starting transfers between devices  54 us (10%)
  other arithmetic  31.8 us (6%)
  local copies, waits for them, and re-layouts  23.4 us (4%)
  blocking collectives  14.2 us (3%)
  between operations  13.9 us (3%)
    reduce_scatter x2, waiting for transfers between devices, attend_step(): lax.psum_scatter(jnp.concatenate((part_q, part_kv), axis=1), 'wide', scat...  190 us
    ppermute x24, waiting for transfers between devices, doubled_up(): lax.ppermute(line, axis, [(d, (d - have) % ways) for d in range(ways)])  67.1 us
    reduce_scatter x2, waiting for transfers between devices, on_device(): lax.psum_scatter(partial_value, 'narrow', scatter_dimension=0, tiled=True)  63.8 us
    ppermute x24, starting transfers between devices, doubled_up(): lax.ppermute(line, axis, [(d, (d - have) % ways) for d in range(ways)])  53.8 us
    dot_general x2, matrix products, attend_step(): jnp.einsum('rgjd,rgcd->rgjc', query, key_cache, preferred_element_type=jn...  24.5 us
    unnamed x21, local copies, waits for them, and re-layouts  21.2 us
    dot_general x2, matrix products, attend_step(): jnp.dot(jnp.concatenate([doubled_up(attended[:, i * 1024:(i + 1) * 1024],...  20.4 us
    dot_general x2, matrix products, attend_step(): part_q = jnp.dot(every, w_q2, preferred_element_type=jnp.float32)  18.7 us
  transfers between devices with their start and end apart: 29, of which 21 were waited for; matrix products, arithmetic and copies ran while one was open for 5% of the time, Pallas kernels for 0%

profile of v1, /device:TPU:0, one launch (start us, length us, event | category | flops | bytes accessed | tf_op | source)
XLA Modules:
  0.0 543.4 jit_solution(9354478611500911644)
XLA Ops:
  7.3 17.5 %copy.69 = bf16[256,8,2,2048]{3,1,2,0:T(8,128)(2,1)} copy(bf16[256,8,2,2048]{3,2,1,0:T(2,128)(2,1)} %bitcast.62) | data formatting | bytes 33554432
  25.3 3.0 all-gather.2.cloned.1.call-done
  28.4 10.5 %fusion.136 = f32[256,4096]{1,0:T(8,128)S(1)} fusion(bf16[256,2048]{1,0:T(8,128)(2,1)} %all-gather.2.cloned.1.call-done, bf16[2048,4096]{1,0:T(8,128)(2,1)} %bitcast.63), kind=kOutput, calls=%fused_computation.258 | convolution fusion | flops 4294967296 | bytes 22020096 | tf_op jit(solution)/shard_map/dot_general | solution.py:45
  39.7 2.6 pad_maximum_fusion
  43.2 94.6 %reduce-scatter.5.cloned.1.call-done = f32[32,4608]{1,0:T(8,128)} async-done(((f32[256,4608]{1,0:T(8,128)}), f32[32,4608]{1,0:T(8,128)}) %reduce-scatter.5.cloned.1.call-update) | async-done | bytes 589840 | tf_op jit(solution)/shard_map/reduce_scatter | solution.py:47
  138.8 1.1 slice_bitcast_fusion.1
  140.7 12.3 %fusion = (f32[32,2,16]{2,1,0:T(2,128)S(1)}, f32[32,2,16,1024]{3,2,1,0:T(8,128)}) fusion(pred[32,1024]{1,0:T(8,128)(4,1)S(1)} %iota_compare_fusion, bf16[32,2,1024,128]{3,2,1,0:T(8,128)(2,1)} %param.13, bf16[32,2,16,64]{3,2,1,0:T(8,128)(2,1)S(1)} %get-tuple-element.9, bf16[32,2,16,64]{3,2,1,0:T(8,128)(2,1)S(1)} %get-tuple-element.8), kind=kOutput, calls=%fused_computation.8 | convolution fusion | flops 272104448 | bytes 21270528 | tf_op jit(solution)/shard_map/rgjd,rgcd->rgjc/dot_general | solution.py:62
  153.0 3.8 fusion.2
  156.9 7.5 %fusion.35 = bf16[32,2,16,128]{3,2,1,0:T(8,128)(2,1)S(1)} fusion(bf16[32,2,1024,128]{3,2,1,0:T(8,128)(2,1)} %param.14, f32[32,2,16,1024]{3,2,1,0:T(8,128)S(1)} %copy-done.1, f32[32,2,16]{2,1,0:T(2,128)S(1)} %get-tuple-element.23, f32[32,2,16]{2,1,0:T(2,128)S(1)} %multiply_maximum_fusion, pred[32,1024]{1,0:T(8,128)(4,1)S(1)} %iota_compare_fusion, ...), kind=kOutput, calls=%fused_computation.44 | convolution fusion | flops 275120128 | bytes 21311488 | tf_op jit(solution)/shard_map/rgjc,rgcd->rgjd/dot_general | solution.py:74
  164.5 3.1 collective-permute-start
  167.6 1.0 collective-permute-start.3
  168.7 2.4 collective-permute-start.6
  172.6 1.9 collective-permute-start.4
  175.5 1.4 collective-permute-start.10
  176.9 1.9 collective-permute-done.1
  178.8 1.0 collective-permute-start.2
  179.8 1.8 collective-permute-done.4
  181.6 1.0 collective-permute-start.5
  182.6 1.7 collective-permute-done.7
  184.3 1.1 collective-permute-start.8
  186.3 1.9 collective-permute-start.11
  188.3 26.6 %collective-permute-done.2 = bf16[128,1024]{1,0:T(8,128)(2,1)S(1)} collective-permute-done((bf16[128,1024]{1,0:T(8,128)(2,1)S(1)}, bf16[128,1024]{1,0:T(8,128)(2,1)S(1)}, u32[]{:S(2)}, u32[]{:S(2)}) %collective-permute-start.2) | collective-permute-done | bytes 262176 | tf_op jit(solution)/shard_map/ppermute | solution.py:15
  214.8 1.8 fusion.89
  216.6 3.8 collective-permute-done.5
  220.4 1.8 fusion.82
  222.3 3.8 collective-permute-done.8
  226.0 1.8 fusion.75
  227.9 2.8 collective-permute-done.11
  230.6 1.8 fusion.68
  232.5 10.2 %fusion.6 = f32[256,2048]{1,0:T(8,128)} fusion(bf16[4096,2048]{1,0:T(8,128)(2,1)} %param.12, bf16[256,1024]{1,0:T(8,128)(2,1)S(1)} %fusion.68, bf16[256,1024]{1,0:T(8,128)(2,1)S(1)} %fusion.75, bf16[256,1024]{1,0:T(8,128)(2,1)S(1)} %fusion.82, bf16[256,1024]{1,0:T(8,128)(2,1)S(1)} %fusion.89), kind=kOutput, calls=%fused_computation.14 | convolution fusion | flops 4303355904 | bytes 20971520 | tf_op jit(solution)/shard_map/dot_general | solution.py:77
  242.8 31.9 %reduce-scatter.7.cloned.1.call-done = f32[64,2048]{1,0:T(8,128)} async-done(((f32[256,2048]{1,0:T(8,128)}), f32[64,2048]{1,0:T(8,128)}) %reduce-scatter.7.cloned.1.call-update) | async-done | bytes 524304 | tf_op jit(solution)/shard_map/reduce_scatter | solution.py:125
  274.7 1.1 add_convert_fusion.2
  275.8 6.8 %all_gather.10 = bf16[128,2048]{1,0:T(8,128)(2,1)S(1)} all-gather(bf16[32,2048]{1,0:T(8,128)(2,1)S(1)} %get-tuple-element.14), channel_id=1, replica_groups=mesh['narrow'=4,'wide'=8] {'narrow'}, dimensions={0}, use_global_device_ids=true | all-gather | bytes 655360 | tf_op jit(solution)/shard_map/all_gather | solution.py:94
  282.6 7.4 %all_gather.11 = bf16[128,2048]{1,0:T(8,128)(2,1)S(1)} all-gather(bf16[32,2048]{1,0:T(8,128)(2,1)S(1)} %get-tuple-element.15), channel_id=1, replica_groups=mesh['narrow'=4,'wide'=8] {'narrow'}, dimensions={0}, use_global_device_ids=true | all-gather | bytes 655360 | tf_op jit(solution)/shard_map/all_gather | solution.py:94
  290.2 8.2 %fusion.138 = f32[256,4096]{1,0:T(8,128)S(1)} fusion(bf16[256,2048]{1,0:T(8,128)(2,1)S(1)} %bitcast.72, bf16[2048,4096]{1,0:T(8,128)(2,1)} %bitcast.64), kind=kOutput, calls=%fused_computation.260 | convolution fusion | flops 4294967296 | bytes 22020096 | tf_op jit(solution)/shard_map/dot_general | solution.py:45
  299.1 2.6 pad_maximum_fusion.1
  301.8 95.8 %reduce-scatter.9.cloned.1.call-done = f32[32,4608]{1,0:T(8,128)} async-done(((f32[256,4608]{1,0:T(8,128)}), f32[32,4608]{1,0:T(8,128)}) %reduce-scatter.9.cloned.1.call-update) | async-done | bytes 589840 | tf_op jit(solution)/shard_map/reduce_scatter | solution.py:47
  398.7 1.1 slice_bitcast_fusion
  400.1 12.3 %fusion.1 = (f32[32,2,16]{2,1,0:T(2,128)S(1)}, f32[32,2,16,1024]{3,2,1,0:T(8,128)}) fusion(pred[32,1024]{1,0:T(8,128)(4,1)S(1)} %iota_compare_fusion, bf16[32,2,1024,128]{3,2,1,0:T(8,128)(2,1)} %param.13, bf16[32,2,16,64]{3,2,1,0:T(8,128)(2,1)S(1)} %get-tuple-element.7, bf16[32,2,16,64]{3,2,1,0:T(8,128)(2,1)S(1)} %get-tuple-element.6), kind=kOutput, calls=%fused_computation.9 | convolution fusion | flops 272104448 | bytes 21270528 | tf_op jit(solution)/shard_map/rgjd,rgcd->rgjc/dot_general | solution.py:62
  413.1 3.9 fusion.3
  417.1 7.3 %fusion.5 = f32[32,2,16,128]{3,2,1,0:T(8,128)S(1)} fusion(bf16[32,2,1024,128]{3,2,1,0:T(8,128)(2,1)} %param.14, f32[32,2,16,1024]{3,2,1,0:T(8,128)S(1)} %copy-done, f32[32,2,16]{2,1,0:T(2,128)S(1)} %add.67, f32[32,2,16]{2,1,0:T(2,128)S(1)} %max.13, pred[32,1024]{1,0:T(8,128)(4,1)S(1)} %iota_compare_fusion), kind=kOutput, calls=%fused_computation.13 | convolution fusion | flops 274726912 | bytes 21536768 | tf_op jit(solution)/shard_map/rgjc,rgcd->rgjd/dot_general | solution.py:74
  424.9 3.1 collective-permute-start.12
  428.6 2.4 collective-permute-start.18
  432.5 1.9 collective-permute-start.16
  434.4 1.1 collective-permute-start.19
  435.5 1.4 collective-permute-start.22
  436.9 1.8 collective-permute-done.13
  438.7 1.4 collective-permute-start.14
  440.1 1.4 collective-permute-done.16
  441.5 1.4 collective-permute-start.17
  442.9 1.3 collective-permute-done.19
  444.2 1.5 collective-permute-start.20
  446.3 20.2 %collective-permute-start.23 = (bf16[128,1024]{1,0:T(8,128)(2,1)S(1)}, bf16[128,1024]{1,0:T(8,128)(2,1)S(1)}, u32[]{:S(2)}, u32[]{:S(2)}) collective-permute-start(bf16[128,1024]{1,0:T(8,128)(2,1)S(1)} %pad_maximum_fusion.12), channel_id=1, source_target_pairs={{0,4},{1,5},{2,6},{3,7},{4,0},{5,1},{6,2},{7,3},{8,12},{9,13},{10,... | collective-permute-start | bytes 786440 | tf_op jit(solution)/shard_map/ppermute | solution.py:15
  466.5 8.9 %collective-permute-done.14 = bf16[128,1024]{1,0:T(8,128)(2,1)S(1)} collective-permute-done((bf16[128,1024]{1,0:T(8,128)(2,1)S(1)}, bf16[128,1024]{1,0:T(8,128)(2,1)S(1)}, u32[]{:S(2)}, u32[]{:S(2)}) %collective-permute-start.14) | collective-permute-done | bytes 262176 | tf_op jit(solution)/shard_map/ppermute | solution.py:15
  475.4 1.8 fusion.61
  477.2 3.8 collective-permute-done.17
  481.0 1.8 fusion.54
  482.9 3.8 collective-permute-done.20
  486.7 1.8 fusion.47
  488.5 2.5 collective-permute-done.23
  490.9 1.8 fusion.40
  492.8 10.2 %fusion.14 = f32[256,2048]{1,0:T(8,128)} fusion(bf16[4096,2048]{1,0:T(8,128)(2,1)} %param.12, bf16[256,1024]{1,0:T(8,128)(2,1)S(1)} %fusion.40, bf16[256,1024]{1,0:T(8,128)(2,1)S(1)} %fusion.47, bf16[256,1024]{1,0:T(8,128)(2,1)S(1)} %fusion.54, bf16[256,1024]{1,0:T(8,128)(2,1)S(1)} %fusion.61), kind=kOutput, calls=%fused_computation.22 | convolution fusion | flops 4303355904 | bytes 20971520 | tf_op jit(solution)/shard_map/dot_general | solution.py:77
  503.0 31.9 %reduce-scatter.11.cloned.1.call-done = f32[64,2048]{1,0:T(8,128)} async-done(((f32[256,2048]{1,0:T(8,128)}), f32[64,2048]{1,0:T(8,128)}) %reduce-scatter.11.cloned.1.call-update) | async-done | bytes 524304 | tf_op jit(solution)/shard_map/reduce_scatter | solution.py:125
  534.9 1.8 add_convert_fusion
  (99 shorter events, 14.7 us)
Async XLA Ops:
  6.5 21.8 %all-gather.2.cloned.1.call-start = ((), (), s32[]{:S(2)}) async-start(), calls=%async_computation.4 | async-start | bytes 1310720 | tf_op jit(solution)/shard_map/all_gather | solution.py:111
  7.3 130.6 %reduce-scatter.5.cloned.1.call-start = ((), (), s32[]{:S(2)}) async-start(), calls=%async_computation.5 | async-start | bytes 5308416 | tf_op jit(solution)/shard_map/reduce_scatter | solution.py:47
  7.3 17.5 %copy-start.2 = (bf16[2048,2,256]{2,1,0:T(2,128)(2,1)S(1)}, bf16[2048,2,256]{2,1,0:T(2,128)(2,1)}, u32[]{:S(2)}) copy-start(bf16[2048,2,256]{2,1,0:T(2,128)(2,1)} %param.11) | copy-start | bytes 6291460
  28.4 10.6 %copy-start.5 = (bf16[256,2048]{1,0:T(8,128)(2,1)S(1)}, bf16[256,2048]{1,0:T(8,128)(2,1)}, u32[]{:S(2)}) copy-start(bf16[256,2048]{1,0:T(8,128)(2,1)} %all-gather.2.cloned.1.call-done) | copy-start | bytes 3145732
  42.2 0.7 copy-start.4
  42.3 232.4 %reduce-scatter.7.cloned.1.call-start = ((), (), s32[]{:S(2)}) async-start(), calls=%async_computation.6 | async-start | bytes 2621440 | tf_op jit(solution)/shard_map/reduce_scatter | solution.py:125
  152.9 3.9 copy-start.1
  164.5 7.1 %collective-permute-start = (bf16[32,1024]{1,0:T(8,128)(2,1)S(1)}, bf16[32,1024]{1,0:T(8,128)(2,1)S(1)}, u32[]{:S(2)}, u32[]{:S(2)}) collective-permute-start(bf16[32,1024]{1,0:T(8,128)(2,1)S(1)} %get-tuple-element.16), channel_id=1, source_target_pairs={{0,7},{1,0},{2,1},{3,2},{4,3},{5,4},{6,5},{7,6},{8,15},{9,8},{10,9... | collective-permute-start | bytes 196616 | tf_op jit(solution)/shard_map/ppermute | solution.py:15
  167.6 4.9 collective-permute-start.3
  168.7 5.8 %collective-permute-start.6 = (bf16[32,1024]{1,0:T(8,128)(2,1)S(1)}, bf16[32,1024]{1,0:T(8,128)(2,1)S(1)}, u32[]{:S(2)}, u32[]{:S(2)}) collective-permute-start(bf16[32,1024]{1,0:T(8,128)(2,1)S(1)} %get-tuple-element.18), channel_id=1, source_target_pairs={{0,7},{1,0},{2,1},{3,2},{4,3},{5,4},{6,5},{7,6},{8,15},{9,8},{10,9... | collective-permute-start | bytes 196616 | tf_op jit(solution)/shard_map/ppermute | solution.py:15
  171.1 4.4 collective-permute-start.9
  171.7 7.1 %collective-permute-start.1 = (bf16[64,1024]{1,0:T(8,128)(2,1)S(1)}, bf16[64,1024]{1,0:T(8,128)(2,1)S(1)}, u32[]{:S(2)}, u32[]{:S(2)}) collective-permute-start(bf16[64,1024]{1,0:T(8,128)(2,1)S(1)} %pad_maximum_fusion.13), channel_id=1, source_target_pairs={{0,6},{1,7},{2,0},{3,1},{4,2},{5,3},{6,4},{7,5},{8,14},{9,15},{10,... | collective-permute-start | bytes 393224 | tf_op jit(solution)/shard_map/ppermute | solution.py:15
  172.6 9.0 %collective-permute-start.4 = (bf16[64,1024]{1,0:T(8,128)(2,1)S(1)}, bf16[64,1024]{1,0:T(8,128)(2,1)S(1)}, u32[]{:S(2)}, u32[]{:S(2)}) collective-permute-start(bf16[64,1024]{1,0:T(8,128)(2,1)S(1)} %pad_maximum_fusion.14), channel_id=1, source_target_pairs={{0,6},{1,7},{2,0},{3,1},{4,2},{5,3},{6,4},{7,5},{8,14},{9,15},{10,... | collective-permute-start | bytes 393224 | tf_op jit(solution)/shard_map/ppermute | solution.py:15
  174.5 9.8 %collective-permute-start.7 = (bf16[64,1024]{1,0:T(8,128)(2,1)S(1)}, bf16[64,1024]{1,0:T(8,128)(2,1)S(1)}, u32[]{:S(2)}, u32[]{:S(2)}) collective-permute-start(bf16[64,1024]{1,0:T(8,128)(2,1)S(1)} %pad_maximum_fusion.15), channel_id=1, source_target_pairs={{0,6},{1,7},{2,0},{3,1},{4,2},{5,3},{6,4},{7,5},{8,14},{9,15},{10,... | collective-permute-start | bytes 393224 | tf_op jit(solution)/shard_map/ppermute | solution.py:15
  175.5 10.8 %collective-permute-start.10 = (bf16[64,1024]{1,0:T(8,128)(2,1)S(1)}, bf16[64,1024]{1,0:T(8,128)(2,1)S(1)}, u32[]{:S(2)}, u32[]{:S(2)}) collective-permute-start(bf16[64,1024]{1,0:T(8,128)(2,1)S(1)} %pad_maximum_fusion.16), channel_id=1, source_target_pairs={{0,6},{1,7},{2,0},{3,1},{4,2},{5,3},{6,4},{7,5},{8,14},{9,15},{10,... | collective-permute-start | bytes 393224 | tf_op jit(solution)/shard_map/ppermute | solution.py:15
  178.8 36.0 %collective-permute-start.2 = (bf16[128,1024]{1,0:T(8,128)(2,1)S(1)}, bf16[128,1024]{1,0:T(8,128)(2,1)S(1)}, u32[]{:S(2)}, u32[]{:S(2)}) collective-permute-start(bf16[128,1024]{1,0:T(8,128)(2,1)S(1)} %pad_maximum_fusion.4), channel_id=1, source_target_pairs={{0,4},{1,5},{2,6},{3,7},{4,0},{5,1},{6,2},{7,3},{8,12},{9,13},{10,... | collective-permute-start | bytes 786440 | tf_op jit(solution)/shard_map/ppermute | solution.py:15
  181.6 38.8 %collective-permute-start.5 = (bf16[128,1024]{1,0:T(8,128)(2,1)S(1)}, bf16[128,1024]{1,0:T(8,128)(2,1)S(1)}, u32[]{:S(2)}, u32[]{:S(2)}) collective-permute-start(bf16[128,1024]{1,0:T(8,128)(2,1)S(1)} %pad_maximum_fusion.5), channel_id=1, source_target_pairs={{0,4},{1,5},{2,6},{3,7},{4,0},{5,1},{6,2},{7,3},{8,12},{9,13},{10,... | collective-permute-start | bytes 786440 | tf_op jit(solution)/shard_map/ppermute | solution.py:15
  184.3 41.7 %collective-permute-start.8 = (bf16[128,1024]{1,0:T(8,128)(2,1)S(1)}, bf16[128,1024]{1,0:T(8,128)(2,1)S(1)}, u32[]{:S(2)}, u32[]{:S(2)}) collective-permute-start(bf16[128,1024]{1,0:T(8,128)(2,1)S(1)} %pad_maximum_fusion.6), channel_id=1, source_target_pairs={{0,4},{1,5},{2,6},{3,7},{4,0},{5,1},{6,2},{7,3},{8,12},{9,13},{10,... | collective-permute-start | bytes 786440 | tf_op jit(solution)/shard_map/ppermute | solution.py:15
  186.3 44.3 %collective-permute-start.11 = (bf16[128,1024]{1,0:T(8,128)(2,1)S(1)}, bf16[128,1024]{1,0:T(8,128)(2,1)S(1)}, u32[]{:S(2)}, u32[]{:S(2)}) collective-permute-start(bf16[128,1024]{1,0:T(8,128)(2,1)S(1)} %pad_maximum_fusion.7), channel_id=1, source_target_pairs={{0,4},{1,5},{2,6},{3,7},{4,0},{5,1},{6,2},{7,3},{8,12},{9,13},{10,... | collective-permute-start | bytes 786440 | tf_op jit(solution)/shard_map/ppermute | solution.py:15
  232.5 42.2 %copy-start.3 = (bf16[64,2048]{1,0:T(8,128)(2,1)S(1)}, bf16[64,2048]{1,0:T(8,128)(2,1)}, u32[]{:S(2)}) copy-start(bf16[64,2048]{1,0:T(8,128)(2,1)} %param.9) | copy-start | bytes 786436
  242.7 154.9 %reduce-scatter.9.cloned.1.call-start = ((), (), s32[]{:S(2)}) async-start(), calls=%async_computation.7 | async-start | bytes 5308416 | tf_op jit(solution)/shard_map/reduce_scatter | solution.py:47
  301.6 233.3 %reduce-scatter.11.cloned.1.call-start = ((), (), s32[]{:S(2)}) async-start(), calls=%async_computation.8 | async-start | bytes 2621440 | tf_op jit(solution)/shard_map/reduce_scatter | solution.py:125
  412.4 4.7 copy-start
  424.9 6.6 %collective-permute-start.12 = (bf16[32,1024]{1,0:T(8,128)(2,1)S(1)}, bf16[32,1024]{1,0:T(8,128)(2,1)S(1)}, u32[]{:S(2)}, u32[]{:S(2)}) collective-permute-start(bf16[32,1024]{1,0:T(8,128)(2,1)S(1)} %get-tuple-element.10), channel_id=1, source_target_pairs={{0,7},{1,0},{2,1},{3,2},{4,3},{5,4},{6,5},{7,6},{8,15},{9,8},{10,9... | collective-permute-start | bytes 196616 | tf_op jit(solution)/shard_map/ppermute | solution.py:15
  428.0 4.5 collective-permute-start.15
  428.6 5.8 %collective-permute-start.18 = (bf16[32,1024]{1,0:T(8,128)(2,1)S(1)}, bf16[32,1024]{1,0:T(8,128)(2,1)S(1)}, u32[]{:S(2)}, u32[]{:S(2)}) collective-permute-start(bf16[32,1024]{1,0:T(8,128)(2,1)S(1)} %get-tuple-element.12), channel_id=1, source_target_pairs={{0,7},{1,0},{2,1},{3,2},{4,3},{5,4},{6,5},{7,6},{8,15},{9,8},{10,9... | collective-permute-start | bytes 196616 | tf_op jit(solution)/shard_map/ppermute | solution.py:15
  430.9 4.6 collective-permute-start.21
  431.5 7.2 %collective-permute-start.13 = (bf16[64,1024]{1,0:T(8,128)(2,1)S(1)}, bf16[64,1024]{1,0:T(8,128)(2,1)S(1)}, u32[]{:S(2)}, u32[]{:S(2)}) collective-permute-start(bf16[64,1024]{1,0:T(8,128)(2,1)S(1)} %pad_maximum_fusion.17), channel_id=1, source_target_pairs={{0,6},{1,7},{2,0},{3,1},{4,2},{5,3},{6,4},{7,5},{8,14},{9,15},{10,... | collective-permute-start | bytes 393224 | tf_op jit(solution)/shard_map/ppermute | solution.py:15
  432.5 9.0 %collective-permute-start.16 = (bf16[64,1024]{1,0:T(8,128)(2,1)S(1)}, bf16[64,1024]{1,0:T(8,128)(2,1)S(1)}, u32[]{:S(2)}, u32[]{:S(2)}) collective-permute-start(bf16[64,1024]{1,0:T(8,128)(2,1)S(1)} %pad_maximum_fusion.18), channel_id=1, source_target_pairs={{0,6},{1,7},{2,0},{3,1},{4,2},{5,3},{6,4},{7,5},{8,14},{9,15},{10,... | collective-permute-start | bytes 393224 | tf_op jit(solution)/shard_map/ppermute | solution.py:15
  434.4 9.8 %collective-permute-start.19 = (bf16[64,1024]{1,0:T(8,128)(2,1)S(1)}, bf16[64,1024]{1,0:T(8,128)(2,1)S(1)}, u32[]{:S(2)}, u32[]{:S(2)}) collective-permute-start(bf16[64,1024]{1,0:T(8,128)(2,1)S(1)} %pad_maximum_fusion.19), channel_id=1, source_target_pairs={{0,6},{1,7},{2,0},{3,1},{4,2},{5,3},{6,4},{7,5},{8,14},{9,15},{10,... | collective-permute-start | bytes 393224 | tf_op jit(solution)/shard_map/ppermute | solution.py:15
  435.5 10.7 %collective-permute-start.22 = (bf16[64,1024]{1,0:T(8,128)(2,1)S(1)}, bf16[64,1024]{1,0:T(8,128)(2,1)S(1)}, u32[]{:S(2)}, u32[]{:S(2)}) collective-permute-start(bf16[64,1024]{1,0:T(8,128)(2,1)S(1)} %pad_maximum_fusion.20), channel_id=1, source_target_pairs={{0,6},{1,7},{2,0},{3,1},{4,2},{5,3},{6,4},{7,5},{8,14},{9,15},{10,... | collective-permute-start | bytes 393224 | tf_op jit(solution)/shard_map/ppermute | solution.py:15
  438.7 36.7 %collective-permute-start.14 = (bf16[128,1024]{1,0:T(8,128)(2,1)S(1)}, bf16[128,1024]{1,0:T(8,128)(2,1)S(1)}, u32[]{:S(2)}, u32[]{:S(2)}) collective-permute-start(bf16[128,1024]{1,0:T(8,128)(2,1)S(1)} %pad_maximum_fusion.9), channel_id=1, source_target_pairs={{0,4},{1,5},{2,6},{3,7},{4,0},{5,1},{6,2},{7,3},{8,12},{9,13},{10,... | collective-permute-start | bytes 786440 | tf_op jit(solution)/shard_map/ppermute | solution.py:15
  441.5 39.5 %collective-permute-start.17 = (bf16[128,1024]{1,0:T(8,128)(2,1)S(1)}, bf16[128,1024]{1,0:T(8,128)(2,1)S(1)}, u32[]{:S(2)}, u32[]{:S(2)}) collective-permute-start(bf16[128,1024]{1,0:T(8,128)(2,1)S(1)} %pad_maximum_fusion.10), channel_id=1, source_target_pairs={{0,4},{1,5},{2,6},{3,7},{4,0},{5,1},{6,2},{7,3},{8,12},{9,13},{10,... | collective-permute-start | bytes 786440 | tf_op jit(solution)/shard_map/ppermute | solution.py:15
  444.2 42.4 %collective-permute-start.20 = (bf16[128,1024]{1,0:T(8,128)(2,1)S(1)}, bf16[128,1024]{1,0:T(8,128)(2,1)S(1)}, u32[]{:S(2)}, u32[]{:S(2)}) collective-permute-start(bf16[128,1024]{1,0:T(8,128)(2,1)S(1)} %pad_maximum_fusion.11), channel_id=1, source_target_pairs={{0,4},{1,5},{2,6},{3,7},{4,0},{5,1},{6,2},{7,3},{8,12},{9,13},{10,... | collective-permute-start | bytes 786440 | tf_op jit(solution)/shard_map/ppermute | solution.py:15
  446.3 44.7 %collective-permute-start.23 = (bf16[128,1024]{1,0:T(8,128)(2,1)S(1)}, bf16[128,1024]{1,0:T(8,128)(2,1)S(1)}, u32[]{:S(2)}, u32[]{:S(2)}) collective-permute-start(bf16[128,1024]{1,0:T(8,128)(2,1)S(1)} %pad_maximum_fusion.12), channel_id=1, source_target_pairs={{0,4},{1,5},{2,6},{3,7},{4,0},{5,1},{6,2},{7,3},{8,12},{9,13},{10,... | collective-permute-start | bytes 786440 | tf_op jit(solution)/shard_map/ppermute | solution.py:15
Sparse Core Ops, SparseCore 0:
  8.9 19.4 all-gather.1
  42.4 95.3 reduce-scatter.4
  242.8 31.8 reduce-scatter.6
  301.8 95.7 reduce-scatter.8
  503.1 31.7 reduce-scatter.10
